TPU v7x, 32 devices: a whole 2x2x4 slice. The times are simulated.
32 devices in a mesh: ctx: 4 (over y, core), row: 8 (over z, x).
Axes of the slice: x: 2, y: 2, z: 4, core: 2. Of those that a mesh axis runs over, the one named last changes fastest.
Arguments:
- queries: bfloat16 [16, 2, 4096], P('row'), may hold values from -400 to 400
- prefix_id: int32 [16], P('row'), may hold values from 0 to 7
- prefix_keys: bfloat16 [8, 1024, 512], P(None, ('ctx', 'row')), may hold values from -8 to 8
- prefix_values: bfloat16 [8, 1024, 512], P(None, ('ctx', 'row')), may hold values from -6 to 6
- pool_keys: bfloat16 [512, 64, 512], P(('ctx', 'row')), may hold values from -5 to 5
- pool_values: bfloat16 [512, 64, 512], P(('ctx', 'row')), may hold values from -6 to 6
- page_table: int32 [16, 32], P('row'), may hold values from 0 to 511, as said below
- suffix_len: int32 [16], P('row'), may hold values from 256 to 2048
- new_keys: bfloat16 [16, 2, 512], P('row'), may hold values from -6.25 to 6.25
- new_values: bfloat16 [16, 2, 512], P('row'), may hold values from -6 to 6
Outputs:
- attended: bfloat16 [16, 2, 4096], P('row')
Inputs may be any that keep to these rules, and one draw needn't show every extreme that they name: `page_table`: the 64 entries of the rows i with one value of i // 2 name different pool pages p with (p // 16) % (8) == i // 2, and together they name all such pages.
All inputs are finite; a program needn't handle non-finite values.
Results may differ from a plain program's by a relative error of at most 0.003.
Values may be sent and summed in bfloat16 or wider, within the bound.
No kernel may reach another device: no remote copies, remote signals or barrier semaphores. Data moves between devices by JAX's collectives and lax.ppermute only.
A program may use at most 64 MiB of HBM per device.

v0:
```python
import math
import jax
import jax.numpy as jnp
from jax import lax
from jax.sharding import PartitionSpec as P

H = 32
KVH = 4
HD = 128
LANES = 128
MASKED_SCORE = -1e30


def block_stats(scores, valid_mask, values, einsum_form):
    block_peak = jnp.max(jnp.where(valid_mask, scores, MASKED_SCORE), axis=-1)
    weights = jnp.where(valid_mask, jnp.exp(scores - block_peak[..., None]), 0.0).astype(
        jnp.bfloat16
    )
    block_total = jnp.sum(weights.astype(jnp.float32), axis=-1)
    block_sum = jnp.einsum(einsum_form, weights, values, preferred_element_type=jnp.float32)
    return (block_peak, block_total, block_sum)


def combine_pair(earlier, later):
    highest = jnp.maximum(earlier[0], later[0])
    left_factor = jnp.exp(earlier[0] - highest)
    right_factor = jnp.exp(later[0] - highest)
    totals = left_factor * earlier[1] + right_factor * later[1]
    sums = left_factor[..., None] * earlier[2] + right_factor[..., None] * later[2]
    return (highest, totals, sums)


def per_device(
    queries,
    prefix_id,
    prefix_keys,
    prefix_values,
    pool_keys,
    pool_values,
    page_table,
    suffix_len,
    new_keys,
    new_values,
):
    rows_dev, step_count, feature_width = queries.shape
    groups = H // KVH
    score_scale = 1.0 / math.sqrt(HD)
    row_count = lax.axis_size("row")
    ctx_count = lax.axis_size("ctx")
    row_index = lax.axis_index("row")
    ctx_index = lax.axis_index("ctx")
    flat_index = ctx_index * row_count + row_index
    own_query = queries.reshape(rows_dev, step_count, KVH, groups, HD)
    slot_count, page_len, kv_width = pool_keys.shape
    slot_ids = flat_index * slot_count + jnp.arange(slot_count, dtype=jnp.int32)
    slot_match = page_table[:, :, None] == slot_ids[None, None, :]
    entry_pos = jnp.arange(page_table.shape[1], dtype=jnp.int32)
    page_of = jnp.sum(jnp.where(slot_match, entry_pos[None, :, None], 0), axis=1)
    owned = jnp.any(slot_match, axis=1)
    token_pos = (
        page_of[:, :, None] * page_len + jnp.arange(page_len, dtype=jnp.int32)[None, None, :]
    )
    live_mask = owned[:, :, None] & (token_pos < suffix_len[:, None, None])
    live_mask = live_mask.reshape(rows_dev, 1, 1, 1, slot_count * page_len)
    flat_keys = pool_keys.reshape(slot_count * page_len, KVH, HD)
    flat_values = pool_values.reshape(slot_count * page_len, KVH, HD)
    suffix_scores = (
        jnp.einsum("rskgd,tkd->rskgt", own_query, flat_keys, preferred_element_type=jnp.float32)
        * score_scale
    )
    suffix_stats = block_stats(suffix_scores, live_mask, flat_values, "rskgt,tkd->rskgd")
    fresh_keys = new_keys.reshape(rows_dev, step_count, KVH, HD)
    fresh_values = new_values.reshape(rows_dev, step_count, KVH, HD)
    fresh_scores = (
        jnp.einsum("rskgd,rtkd->rskgt", own_query, fresh_keys, preferred_element_type=jnp.float32)
        * score_scale
    )
    causal = jnp.arange(step_count)[None, :] <= jnp.arange(step_count)[:, None]
    causal = causal.reshape(1, step_count, 1, 1, step_count)
    fresh_stats = block_stats(fresh_scores, causal, fresh_values, "rskgt,rtkd->rskgd")
    query_cols = step_count * feature_width
    id_cols = jnp.broadcast_to(prefix_id.astype(jnp.bfloat16)[:, None], (rows_dev, LANES))
    packed = jnp.concatenate([queries.reshape(rows_dev, query_cols), id_cols], axis=1)
    gathered = lax.all_gather(packed, "row", axis=0, tiled=True)
    total_rows = gathered.shape[0]
    every_query = gathered[:, :query_cols].reshape(total_rows, step_count, KVH, groups, HD)
    every_prefix = gathered[:, query_cols].astype(jnp.int32)
    span_len = prefix_keys.shape[1]
    row_keys = jnp.take(prefix_keys, every_prefix, axis=0).reshape(total_rows, span_len, KVH, HD)
    row_values = jnp.take(prefix_values, every_prefix, axis=0).reshape(
        total_rows, span_len, KVH, HD
    )
    prefix_scores = (
        jnp.einsum("rskgd,rtkd->rskgt", every_query, row_keys, preferred_element_type=jnp.float32)
        * score_scale
    )
    always = jnp.ones((1, 1, 1, 1, span_len), dtype=bool)
    prefix_stats = block_stats(prefix_scores, always, row_values, "rskgt,rtkd->rskgd")
    row_start = row_index * rows_dev
    own_prefix = tuple(
        (lax.dynamic_slice_in_dim(member, row_start, rows_dev, 0) for member in prefix_stats)
    )
    own_merged = combine_pair(own_prefix, suffix_stats)
    peak_all, total_all, sum_all = tuple(
        (
            lax.dynamic_update_slice_in_dim(whole_arr, piece_arr, row_start, 0)
            for whole_arr, piece_arr in zip(prefix_stats, own_merged)
        )
    )
    units = rows_dev * step_count * H
    share = units // ctx_count
    pt_rows = -(-2 * share // LANES)
    peak_u = peak_all.reshape(row_count, ctx_count, share)
    total_u = total_all.reshape(row_count, ctx_count, share)
    sum_u = sum_all.reshape(row_count, ctx_count, share, HD)
    pt = jnp.concatenate([peak_u, total_u], axis=-1)
    pt = jnp.pad(pt, ((0, 0), (0, 0), (0, pt_rows * LANES - 2 * share)))
    pt = pt.reshape(row_count, ctx_count, pt_rows, LANES)
    outgoing = jnp.concatenate([sum_u, pt], axis=2)
    outgoing = jnp.swapaxes(outgoing, 0, 1).reshape(ctx_count * row_count, share + pt_rows, LANES)
    incoming = lax.all_to_all(outgoing, ("ctx", "row"), split_axis=0, concat_axis=0, tiled=True)
    sources = incoming.shape[0]
    got_sum = incoming[:, :share, :]
    got_pt = incoming[:, share:, :].reshape(sources, pt_rows * LANES)
    got_peak = got_pt[:, :share]
    got_total = got_pt[:, share : 2 * share]
    unit_start = ctx_index * share
    fresh_peak = lax.dynamic_slice_in_dim(fresh_stats[0].reshape(units), unit_start, share)
    fresh_total = lax.dynamic_slice_in_dim(fresh_stats[1].reshape(units), unit_start, share)
    fresh_sum = lax.dynamic_slice_in_dim(fresh_stats[2].reshape(units, HD), unit_start, share)
    top = jnp.maximum(jnp.max(got_peak, axis=0), fresh_peak)
    factor = jnp.exp(got_peak - top[None])
    fresh_factor = jnp.exp(fresh_peak - top)
    denom = jnp.sum(factor * got_total, axis=0) + fresh_factor * fresh_total
    numer = jnp.sum(factor[..., None] * got_sum, axis=0) + fresh_factor[..., None] * fresh_sum
    result = (numer / denom[..., None]).astype(jnp.bfloat16)
    whole = lax.all_gather(result, "ctx", axis=0, tiled=True)
    return whole.reshape(rows_dev, step_count, H * HD)


def solution(mesh):
    in_specs = (
        P("row", None, None),
        P("row"),
        P(None, ("ctx", "row"), None),
        P(None, ("ctx", "row"), None),
        P(("ctx", "row"), None, None),
        P(("ctx", "row"), None, None),
        P("row", None),
        P("row"),
        P("row", None, None),
        P("row", None, None),
    )
    out_specs = P("row", None, None)
    return jax.shard_map(
        per_device, mesh=mesh, in_specs=in_specs, out_specs=out_specs, check_vma=False
    )
```

profile of v0, /device:TPU:0, one launch (start us, length us, event | category | flops | bytes accessed | tf_op | source)
XLA Modules:
  0.0 77.9 jit_solution(5196668622109800049)
XLA Ops:
  0.0 0.7 convert_element_type.32
  0.7 0.8 %copy.117 = bf16[1,2,2,4096]{3,1,2,0:T(2,128)(2,1)S(1)} copy(bf16[1,2,2,4096]{3,2,1,0:T(2,128)(2,1)} %bitcast.69) | data formatting | bytes 65536
  1.6 32.5 %all-gather = bf16[8,2,8320]{2,1,0:T(2,128)(2,1)S(1)} all-gather(bf16[1,2,8320]{2,1,0:T(2,128)(2,1)S(1)} %maximum_bitcast_fusion.1), channel_id=1, replica_groups=mesh['ctx'=4,'row'=8] {'row'}, dimensions={0}, use_global_device_ids=true | all-gather | bytes 299520 | tf_op jit(solution)/shard_map/all_gather | solution.py:84
  34.2 0.1 reshape.165
  34.3 0.1 convert_reduce_fusion.3
  34.5 0.7 copy-done.10
  35.1 0.2 compare_reduce_fusion
  35.3 0.2 fusion.16
  35.6 0.6 gather_fusion
  36.2 0.4 copy-done.3
  36.5 0.6 gather_fusion.1
  37.1 0.2 broadcast_select_fusion.1
  37.3 0.1 reshape.127
  37.5 0.1 reshape.128
  37.6 0.5 fusion.22
  38.1 0.5 convert_reduce_fusion.1
  38.6 0.3 fusion.10
  39.0 0.1 and.21
  39.2 0.1 add.71
  39.3 0.5 copy-done.1
  39.8 0.3 reshape.130
  40.1 0.6 copy-done.11
  40.7 0.1 compare_and_fusion
  40.8 0.5 select_reduce_fusion
  41.4 0.9 %convert_reduce_fusion = (f32[2,2,4,8]{3,1,0,2:T(2,128)S(1)}, bf16[2,2,4,8,1024]{4,3,1,0,2:T(8,128)(2,1)}) fusion(f32[2,2,4,8,1024]{4,3,1,0,2:T(8,128)S(1)} %get-tuple-element.23, f32[2,2,4,8]{3,1,0,2:T(2,128)S(1)} %get-tuple-element.22, pred[2,1024]{1,0:T(4,128)(4,1)S(1)} %compare_and_fusion), kind=kLoop, calls=%fused_computation.22 | loop fusion | flops 655232 | bytes 789504 | tf_op jit(solution)/shard_map/reduce_sum | solution.py:19
  42.2 0.6 fusion.19
  42.9 0.1 reshape.135
  43.0 0.1 reshape.134
  43.2 0.3 reshape.132
  43.5 0.4 copy-done.7
  43.9 1.2 %fusion.4 = f32[16,2,4,8,128]{4,3,1,2,0:T(8,128)S(1)} fusion(f32[16,2,4,8,128]{4,3,1,2,0:T(8,128)S(1)} %copy.164, s32[]{:T(128)S(6)} %select_n.41, bf16[1024,4,128,1,1]{2,1,0,4,3:T(4,128)(2,1)S(1)} %bitcast.63, bf16[2,2,4,8,1024]{4,3,1,0,2:T(8,128)(2,1)} %get-tuple-element.16, f32[16,4,128,2,8]{2,4,3,1,0:T(8,128)S(1)} %fusion.10, ...), kind=kOutput, calls=%fused_computation.10 | convolution fusion | flops 33603584 | bytes 1458180 | tf_op jit(solution)/shard_map/rskgt,tkd->rskgd/dot_general | solution.py:20
  45.2 0.1 select_maximum_fusion
  45.3 0.3 copy.161
  45.7 1.2 %copy.96 = f32[32,33,128]{2,1,0:T(8,128)} copy(f32[32,33,128]{2,0,1:T(8,128)S(1)} %bitcast.59) | data formatting | bytes 1081344 | tf_op jit(solution)/shard_map/reshape | solution.py:120
  46.8 5.5 %all-to-all-start = ((f32[32,33,128]{2,1,0:T(8,128)}), f32[32,33,128]{2,1,0:T(8,128)S(1)}, u32[]{:S(2)}, u32[]{:S(2)}) async-start(f32[32,33,128]{2,1,0:T(8,128)} %copy.96), calls=%async_computation | async-start | bytes 1310720 | tf_op jit(solution)/shard_map/all_to_all | solution.py:121
  52.4 0.3 select_reduce_fusion.1
  52.7 0.1 reshape.140
  52.8 0.1 convert_reduce_fusion.2
  52.9 0.2 convolution_bitcast_fusion
  53.1 0.1 reshape.143
  53.2 18.3 %all-to-all-done = f32[32,33,128]{2,1,0:T(8,128)S(1)} async-done(((f32[32,33,128]{2,1,0:T(8,128)}), f32[32,33,128]{2,1,0:T(8,128)S(1)}, u32[]{:S(2)}, u32[]{:S(2)}) %all-to-all-start) | async-done | bytes 540704 | tf_op jit(solution)/shard_map/all_to_all | solution.py:121
  71.6 0.1 dynamic-slice_maximum_fusion
  71.6 0.1 fusion.17
  71.7 0.1 multiply_add_fusion
  71.8 0.2 fusion.8
  72.0 0.1 divide_convert_fusion
  72.1 5.2 %all_gather.7 = bf16[128,128]{1,0:T(8,128)(2,1)S(1)} all-gather(bf16[32,128]{1,0:T(8,128)(2,1)S(1)} %divide_convert_fusion), channel_id=1, replica_groups=mesh['ctx'=4,'row'=8] {'ctx'}, dimensions={0}, use_global_device_ids=true | all-gather | bytes 40960 | tf_op jit(solution)/shard_map/all_gather | solution.py:137
  77.3 0.6 reshape.144
  (46 shorter events, 0.8 us)
Async XLA Ops:
  0.0 35.6 %copy-start = (bf16[8,32,512]{2,1,0:T(8,128)(2,1)S(1)}, bf16[8,32,512]{2,1,0:T(8,128)(2,1)}, u32[]{:S(2)}) copy-start(bf16[8,32,512]{2,1,0:T(8,128)(2,1)} %param.15) | copy-start | bytes 786436
  34.4 1.1 %copy-start.4 = (bf16[2,2,4096]{2,1,0:T(2,128)(2,1)S(1)}, bf16[2,2,4096]{2,1,0:T(2,128)(2,1)}, u32[]{:S(2)}) copy-start(bf16[2,2,4096]{2,1,0:T(2,128)(2,1)} %param.12) | copy-start | bytes 98308
  34.4 0.7 copy-start.10
  35.5 5.3 %copy-start.5 = (bf16[2,2,4,8,128]{4,3,2,1,0:T(8,128)(2,1)}, bf16[2,2,4,8,128]{4,3,2,1,0:T(8,128)(2,1)S(1)}, u32[]{:S(2)}) copy-start(bf16[2,2,4,8,128]{4,3,2,1,0:T(8,128)(2,1)S(1)} %reshape.131) | copy-start | bytes 98308
  35.6 1.0 %copy-start.3 = (bf16[8,32,512]{2,1,0:T(8,128)(2,1)S(1)}, bf16[8,32,512]{2,1,0:T(8,128)(2,1)}, u32[]{:S(2)}) copy-start(bf16[8,32,512]{2,1,0:T(8,128)(2,1)} %param.14) | copy-start | bytes 786436
  38.6 1.2 %copy-start.1 = (bf16[16,64,512]{2,1,0:T(8,128)(2,1)S(1)}, bf16[16,64,512]{2,1,0:T(8,128)(2,1)}, u32[]{:S(2)}) copy-start(bf16[16,64,512]{2,1,0:T(8,128)(2,1)} %param.16) | copy-start | bytes 3145732
  40.1 0.7 copy-start.11
  41.4 1.8 %copy-start.2 = (bf16[16,64,512]{2,1,0:T(8,128)(2,1)S(1)}, bf16[16,64,512]{2,1,0:T(8,128)(2,1)}, u32[]{:S(2)}) copy-start(bf16[16,64,512]{2,1,0:T(8,128)(2,1)} %param.17) | copy-start | bytes 3145732
  43.2 0.7 copy-start.7
  43.2 0.7 copy-start.8
  46.8 5.6 %copy-start.6 = (bf16[2,2,4,8,128]{4,3,2,1,0:T(8,128)(2,1)S(1)}, bf16[2,2,4,8,128]{4,3,2,1,0:T(8,128)(2,1)}, u32[]{:S(2)}) copy-start(bf16[2,2,4,8,128]{4,3,2,1,0:T(8,128)(2,1)} %copy-done.5) | copy-start | bytes 98308
  46.8 5.6 %copy-start.12 = (bf16[2,2,512]{2,1,0:T(2,128)(2,1)S(1)}, bf16[2,2,512]{2,1,0:T(2,128)(2,1)}, u32[]{:S(2)}) copy-start(bf16[2,2,512]{2,1,0:T(2,128)(2,1)} %param.20) | copy-start | bytes 12292
  46.8 6.1 %copy-start.9 = (bf16[2,2,512]{2,1,0:T(2,128)(2,1)S(1)}, bf16[2,2,512]{2,1,0:T(2,128)(2,1)}, u32[]{:S(2)}) copy-start(bf16[2,2,512]{2,1,0:T(2,128)(2,1)} %param.21) | copy-start | bytes 12292
  46.8 24.7 %all-to-all-start = ((f32[32,33,128]{2,1,0:T(8,128)}), f32[32,33,128]{2,1,0:T(8,128)S(1)}, u32[]{:S(2)}, u32[]{:S(2)}) async-start(f32[32,33,128]{2,1,0:T(8,128)} %copy.96), calls=%async_computation | async-start | bytes 1310720 | tf_op jit(solution)/shard_map/all_to_all | solution.py:121
where the time goes:
time: 78.4 us; the launch traced here: 77.9 us
  blocking collectives  37.7 us (48%)
  waiting for transfers between devices  18.3 us (23%)
  local copies, waits for them, and re-layouts  8.64 us (11%)
  starting transfers between devices  5.54 us (7%)
  other arithmetic  4.24 us (5%)
  matrix products  3.09 us (4%)
    all_gather x1, blocking collectives, per_device(): gathered = lax.all_gather(packed, 'row', axis=0, tiled=True)  32.5 us
    all_to_all x1, waiting for transfers between devices, per_device(): lax.all_to_all(outgoing, ('ctx', 'row'), split_axis=0, concat_axis=0, til...  18.3 us
    all_to_all x1, starting transfers between devices, per_device(): lax.all_to_all(outgoing, ('ctx', 'row'), split_axis=0, concat_axis=0, til...  5.54 us
    all_gather x1, blocking collectives, per_device(): whole = lax.all_gather(result, 'ctx', axis=0, tiled=True)  5.18 us
    unnamed x31, local copies, waits for them, and re-layouts  3.59 us
    dot_general x3, matrix products, block_stats(): jnp.einsum(einsum_form, weights, values, preferred_element_type=jnp.float32)  1.75 us
  transfers between devices with their start and end apart: 1, of which 1 were waited for; matrix products, arithmetic and copies ran while one was open for 1% of the time, Pallas kernels for 0%

commit v1 on v0

--- a/solution.py
+++ b/solution.py
@@ -9,6 +9,19 @@
 HD = 128
 LANES = 128
 MASKED_SCORE = -1e30
+
+
+def gather_around(x, axis, dim):
+    ways = lax.axis_size(axis)
+    up = [(d, (d + 1) % ways) for d in range(ways)]
+    down = [(d, (d - 1) % ways) for d in range(ways)]
+    earlier, later = ([x], [x])
+    for _ in range(ways // 2):
+        earlier.append(lax.ppermute(earlier[-1], axis, up))
+    for _ in range((ways - 1) // 2):
+        later.append(lax.ppermute(later[-1], axis, down))
+    line = jnp.concatenate([*earlier[::-1], *later[1:]], axis=dim)
+    return jnp.roll(line, (lax.axis_index(axis) - ways // 2) * x.shape[dim], axis=dim)
 
 
 def block_stats(scores, valid_mask, values, einsum_form):
@@ -81,7 +94,7 @@
     query_cols = step_count * feature_width
     id_cols = jnp.broadcast_to(prefix_id.astype(jnp.bfloat16)[:, None], (rows_dev, LANES))
     packed = jnp.concatenate([queries.reshape(rows_dev, query_cols), id_cols], axis=1)
-    gathered = lax.all_gather(packed, "row", axis=0, tiled=True)
+    gathered = gather_around(packed, "row", 0)
     total_rows = gathered.shape[0]
     every_query = gathered[:, :query_cols].reshape(total_rows, step_count, KVH, groups, HD)
     every_prefix = gathered[:, query_cols].astype(jnp.int32)

time: 78.4 us -> 68.2 us (0.87)
  blocking collectives: 37.7 us -> 5.18 us
  starting transfers between devices: 5.54 us -> 18.4 us
  waiting for transfers between devices: 18.3 us -> 25.3 us
  local copies, waits for them, and re-layouts: 8.64 us -> 13.3 us
  other arithmetic: 4.24 us -> 3.13 us
  matrix products: 3.09 us -> 2.14 us
    all_gather x1 -> x0, blocking collectives: 32.5 us -> none  [per_device(): gathered = lax.all_gather(packed, 'row', axis=0, tiled=True)]
    ppermute x0 -> x7, starting transfers between devices: none -> 15.7 us  [the longest x3 12.7 us: gather_around(): later.append(lax.ppermute(later[-1], axis, down))]
    ppermute x0 -> x7, waiting for transfers between devices: none -> 6.98 us  [the longest x4 6.27 us: gather_around(): earlier.append(lax.ppermute(earlier[-1], axis, up))]
    concatenate x0 -> x1, local copies, waits for them, and re-layouts: none -> 3.19 us  [gather_around(): jnp.roll(line, (lax.axis_index(axis) - ways // 2) * x.shape[dim], axis=dim)]
    all_to_all x1, starting transfers between devices: 5.54 us -> 2.75 us  [per_device(): lax.all_to_all(outgoing, ('ctx', 'row'), split_axis=0, concat_axis=0, til...]
    reshape x1, local copies, waits for them, and re-layouts: 0.27 us -> 1.35 us  [per_device(): flat_keys = pool_keys.reshape(slot_count * page_len, KVH, HD)]
    dot_general x3, matrix products: 1.75 us -> 0.81 us  [block_stats(): jnp.einsum(einsum_form, weights, values, preferred_element_type=jnp.float32)]
    reshape x1, local copies, waits for them, and re-layouts: 0.29 us -> 1.13 us  [per_device(): flat_values = pool_values.reshape(slot_count * page_len, KVH, HD)]
  transfers between devices with their start and end apart: 1 -> 8, of which waited for: 1 -> 6; matrix products, arithmetic and copies ran while one was open for 1% -> 7% of each run, Pallas kernels for 0% -> 0%
where the time goes in v1:
time: 68.2 us; the launch traced here: 67.8 us
  waiting for transfers between devices  25.3 us (37%)
  starting transfers between devices  18.4 us (27%)
  local copies, waits for them, and re-layouts  13.3 us (20%)
  blocking collectives  5.18 us (8%)
  other arithmetic  3.13 us (5%)
  matrix products  2.14 us (3%)
    all_to_all x1, waiting for transfers between devices, per_device(): lax.all_to_all(outgoing, ('ctx', 'row'), split_axis=0, concat_axis=0, til...  18.3 us
    ppermute x3, starting transfers between devices, gather_around(): later.append(lax.ppermute(later[-1], axis, down))  12.7 us
    ppermute x4, waiting for transfers between devices, gather_around(): earlier.append(lax.ppermute(earlier[-1], axis, up))  6.27 us
    all_gather x1, blocking collectives, per_device(): whole = lax.all_gather(result, 'ctx', axis=0, tiled=True)  5.18 us
    concatenate x1, local copies, waits for them, and re-layouts, gather_around(): jnp.roll(line, (lax.axis_index(axis) - ways // 2) * x.shape[dim], axis=dim)  3.19 us
    unnamed x22, local copies, waits for them, and re-layouts  3.11 us
    ppermute x4, starting transfers between devices, gather_around(): earlier.append(lax.ppermute(earlier[-1], axis, up))  3 us
    all_to_all x1, starting transfers between devices, per_device(): lax.all_to_all(outgoing, ('ctx', 'row'), split_axis=0, concat_axis=0, til...  2.75 us
  transfers between devices with their start and end apart: 8, of which 6 were waited for; matrix products, arithmetic and copies ran while one was open for 7% of the time, Pallas kernels for 0%

profile of v1, /device:TPU:0, one launch (start us, length us, event | category | flops | bytes accessed | tf_op | source)
XLA Modules:
  0.0 67.8 jit_solution(7213206947805654114)
XLA Ops:
  0.0 0.7 %convert_element_type.32 = bf16[2]{0:T(256)(128)(2,1)S(1)} convert(s32[2]{0:T(128)} %param.13) | non-fusion elementwise | flops 2 | bytes 12 | tf_op jit(solution)/shard_map/convert_element_type | solution.py:95
  0.7 0.8 %copy.117 = bf16[1,2,2,4096]{3,1,2,0:T(2,128)(2,1)S(1)} copy(bf16[1,2,2,4096]{3,2,1,0:T(2,128)(2,1)} %bitcast.67) | data formatting | bytes 65536
  1.6 3.0 %collective-permute-start = (bf16[2,8320]{1,0:T(2,128)(2,1)S(1)}, bf16[2,8320]{1,0:T(2,128)(2,1)S(1)}, u32[]{:S(2)}, u32[]{:S(2)}) collective-permute-start(bf16[2,8320]{1,0:T(2,128)(2,1)S(1)} %pad_maximum_fusion), channel_id=1, source_target_pairs={{0,1},{1,2},{2,3},{3,4},{4,5},{5,6},{6,7},{7,0},{8,9},{9,10},{10,1... | collective-permute-start | bytes 99848 | tf_op jit(solution)/shard_map/ppermute | solution.py:20
  4.6 3.1 %collective-permute-start.4 = (bf16[2,8320]{1,0:T(2,128)(2,1)S(1)}, bf16[2,8320]{1,0:T(2,128)(2,1)S(1)}, u32[]{:S(2)}, u32[]{:S(2)}) collective-permute-start(bf16[2,8320]{1,0:T(2,128)(2,1)S(1)} %pad_maximum_fusion), channel_id=1, source_target_pairs={{0,7},{1,0},{2,1},{3,2},{4,3},{5,4},{6,5},{7,6},{8,15},{9,8},{10,9... | collective-permute-start | bytes 99848 | tf_op jit(solution)/shard_map/ppermute | solution.py:22
  7.7 0.7 copy-done.6
  8.4 0.2 fusion.16
  8.6 0.2 compare_reduce_fusion
  8.8 0.1 and.28
  9.2 0.4 collective-permute-done
  9.5 0.2 copy-done.7
  9.9 1.3 %reshape.130 = bf16[1024,4,128]{2,1,0:T(4,128)(2,1)S(1)} reshape(bf16[16,64,512]{2,1,0:T(8,128)(2,1)} %param.16) | data formatting | bytes 2097152 | tf_op jit(solution)/shard_map/reshape | solution.py:78
  11.2 4.6 %collective-permute-start.5 = (bf16[2,8320]{1,0:T(2,128)(2,1)S(1)}, bf16[2,8320]{1,0:T(2,128)(2,1)S(1)}, u32[]{:S(2)}, u32[]{:S(2)}) collective-permute-start(bf16[2,8320]{1,0:T(2,128)(2,1)S(1)} %collective-permute-done.4), channel_id=1, source_target_pairs={{0,7},{1,0},{2,1},{3,2},{4,3},{5,4},{6,5},{7,6},{8,15},{9,8},{10,9... | collective-permute-start | bytes 99848 | tf_op jit(solution)/shard_map/ppermute | solution.py:22
  15.8 0.4 collective-permute-done.1
  16.2 0.5 select_reduce_fusion
  16.7 0.7 %collective-permute-done.5 = bf16[2,8320]{1,0:T(2,128)(2,1)S(1)} collective-permute-done((bf16[2,8320]{1,0:T(2,128)(2,1)S(1)}, bf16[2,8320]{1,0:T(2,128)(2,1)S(1)}, u32[]{:S(2)}, u32[]{:S(2)}) %collective-permute-start.5) | collective-permute-done | bytes 33312 | tf_op jit(solution)/shard_map/ppermute | solution.py:22
  17.4 5.0 %collective-permute-start.6 = (bf16[2,8320]{1,0:T(2,128)(2,1)S(1)}, bf16[2,8320]{1,0:T(2,128)(2,1)S(1)}, u32[]{:S(2)}, u32[]{:S(2)}) collective-permute-start(bf16[2,8320]{1,0:T(2,128)(2,1)S(1)} %collective-permute-done.5), channel_id=1, source_target_pairs={{0,7},{1,0},{2,1},{3,2},{4,3},{5,4},{6,5},{7,6},{8,15},{9,8},{10,9... | collective-permute-start | bytes 99848 | tf_op jit(solution)/shard_map/ppermute | solution.py:22
  22.4 0.4 collective-permute-done.2
  22.8 0.3 convert_reduce_fusion
  23.1 1.1 %reshape.132 = bf16[1024,4,128]{2,1,0:T(4,128)(2,1)} reshape(bf16[16,64,512]{2,1,0:T(8,128)(2,1)S(1)} %copy-done.1) | data formatting | bytes 2097152 | tf_op jit(solution)/shard_map/reshape | solution.py:79
  24.2 5.2 %collective-permute-done.3 = bf16[2,8320]{1,0:T(2,128)(2,1)S(1)} collective-permute-done((bf16[2,8320]{1,0:T(2,128)(2,1)S(1)}, bf16[2,8320]{1,0:T(2,128)(2,1)S(1)}, u32[]{:S(2)}, u32[]{:S(2)}) %collective-permute-start.3) | collective-permute-done | bytes 33312 | tf_op jit(solution)/shard_map/ppermute | solution.py:20
  29.4 3.2 %concatenate.16 = bf16[32,8320]{1,0:T(8,128)(2,1)S(1)} concatenate(bf16[2,8320]{1,0:T(2,128)(2,1)S(1)} %collective-permute-done.3, bf16[2,8320]{1,0:T(2,128)(2,1)S(1)} %collective-permute-done.2, bf16[2,8320]{1,0:T(2,128)(2,1)S(1)} %collective-permute-done.1, bf16[2,8320]{1,0:T(2,128)(2,1)S(1)} %collective-permute-done, bf16[2,8320]{1,0:T(2,128)(2,1)S(1)} %pad_maximum_fusion, ...), dimensions={0} | concatenate | bytes 1064960 | tf_op jit(solution)/shard_map/jit(_roll_dynamic)/concatenate | solution.py:24
  32.6 0.2 convert_reduce_fusion.3
  32.9 0.6 gather_fusion
  33.5 0.4 copy-done.3
  33.9 0.6 gather_fusion.1
  34.5 0.2 broadcast_select_fusion.1
  34.6 0.1 reshape.127
  34.8 0.1 reshape.128
  34.9 0.5 fusion.22
  35.5 0.5 convert_reduce_fusion.1
  35.9 0.3 fusion.10
  36.3 0.1 reshape.135
  36.4 0.1 reshape.134
  36.6 0.9 %copy-done.2 = bf16[1024,4,128]{2,1,0:T(4,128)(2,1)S(1)} copy-done((bf16[1024,4,128]{2,1,0:T(4,128)(2,1)S(1)}, bf16[1024,4,128]{2,1,0:T(4,128)(2,1)}, u32[]{:S(2)}) %copy-start.2) | copy-done | bytes 1048600
  37.5 0.3 fusion.4
  38.0 0.3 copy.161
  38.3 1.2 %copy.96 = f32[32,33,128]{2,1,0:T(8,128)} copy(f32[32,33,128]{2,0,1:T(8,128)S(1)} %bitcast.57) | data formatting | bytes 1081344 | tf_op jit(solution)/shard_map/reshape | solution.py:133
  39.5 2.7 %all-to-all-start = ((f32[32,33,128]{2,1,0:T(8,128)}), f32[32,33,128]{2,1,0:T(8,128)S(1)}, u32[]{:S(2)}, u32[]{:S(2)}) async-start(f32[32,33,128]{2,1,0:T(8,128)} %copy.96), calls=%async_computation | async-start | bytes 1310720 | tf_op jit(solution)/shard_map/all_to_all | solution.py:134
  42.2 0.3 select_reduce_fusion.1
  42.5 0.1 reshape.140
  42.6 0.1 convert_reduce_fusion.2
  42.7 0.2 convolution_bitcast_fusion
  43.0 0.1 reshape.143
  43.1 18.3 %all-to-all-done = f32[32,33,128]{2,1,0:T(8,128)S(1)} async-done(((f32[32,33,128]{2,1,0:T(8,128)}), f32[32,33,128]{2,1,0:T(8,128)S(1)}, u32[]{:S(2)}, u32[]{:S(2)}) %all-to-all-start) | async-done | bytes 540704 | tf_op jit(solution)/shard_map/all_to_all | solution.py:134
  61.5 0.1 fusion.17
  61.7 0.2 fusion.8
  62.0 5.2 %all_gather.3 = bf16[128,128]{1,0:T(8,128)(2,1)S(1)} all-gather(bf16[32,128]{1,0:T(8,128)(2,1)S(1)} %divide_convert_fusion), channel_id=1, replica_groups=mesh['ctx'=4,'row'=8] {'ctx'}, dimensions={0}, use_global_device_ids=true | all-gather | bytes 40960 | tf_op jit(solution)/shard_map/all_gather | solution.py:150
  67.2 0.6 reshape.144
  (51 shorter events, 1.3 us)
Async XLA Ops:
  0.0 32.9 %copy-start = (bf16[8,32,512]{2,1,0:T(8,128)(2,1)S(1)}, bf16[8,32,512]{2,1,0:T(8,128)(2,1)}, u32[]{:S(2)}) copy-start(bf16[8,32,512]{2,1,0:T(8,128)(2,1)} %param.15) | copy-start | bytes 786436
  1.6 7.9 %collective-permute-start = (bf16[2,8320]{1,0:T(2,128)(2,1)S(1)}, bf16[2,8320]{1,0:T(2,128)(2,1)S(1)}, u32[]{:S(2)}, u32[]{:S(2)}) collective-permute-start(bf16[2,8320]{1,0:T(2,128)(2,1)S(1)} %pad_maximum_fusion), channel_id=1, source_target_pairs={{0,1},{1,2},{2,3},{3,4},{4,5},{5,6},{6,7},{7,0},{8,9},{9,10},{10,1... | collective-permute-start | bytes 99848 | tf_op jit(solution)/shard_map/ppermute | solution.py:20
  4.6 6.6 %collective-permute-start.4 = (bf16[2,8320]{1,0:T(2,128)(2,1)S(1)}, bf16[2,8320]{1,0:T(2,128)(2,1)S(1)}, u32[]{:S(2)}, u32[]{:S(2)}) collective-permute-start(bf16[2,8320]{1,0:T(2,128)(2,1)S(1)} %pad_maximum_fusion), channel_id=1, source_target_pairs={{0,7},{1,0},{2,1},{3,2},{4,3},{5,4},{6,5},{7,6},{8,15},{9,8},{10,9... | collective-permute-start | bytes 99848 | tf_op jit(solution)/shard_map/ppermute | solution.py:22
  7.7 0.7 %copy-start.6 = (s32[2,32]{1,0:T(2,128)S(1)}, s32[2,32]{1,0:T(2,128)}, u32[]{:S(2)}) copy-start(s32[2,32]{1,0:T(2,128)} %param.18) | copy-start | bytes 772
  9.0 0.8 %copy-start.4 = (bf16[2,2,4096]{2,1,0:T(2,128)(2,1)S(1)}, bf16[2,2,4096]{2,1,0:T(2,128)(2,1)}, u32[]{:S(2)}) copy-start(bf16[2,2,4096]{2,1,0:T(2,128)(2,1)} %param.12) | copy-start | bytes 98308
  9.1 0.7 copy-start.7
  9.5 6.6 %collective-permute-start.1 = (bf16[2,8320]{1,0:T(2,128)(2,1)S(1)}, bf16[2,8320]{1,0:T(2,128)(2,1)S(1)}, u32[]{:S(2)}, u32[]{:S(2)}) collective-permute-start(bf16[2,8320]{1,0:T(2,128)(2,1)S(1)} %collective-permute-done), channel_id=1, source_target_pairs={{0,1},{1,2},{2,3},{3,4},{4,5},{5,6},{6,7},{7,0},{8,9},{9,10},{10,1... | collective-permute-start | bytes 99848 | tf_op jit(solution)/shard_map/ppermute | solution.py:20
  11.2 6.2 %collective-permute-start.5 = (bf16[2,8320]{1,0:T(2,128)(2,1)S(1)}, bf16[2,8320]{1,0:T(2,128)(2,1)S(1)}, u32[]{:S(2)}, u32[]{:S(2)}) collective-permute-start(bf16[2,8320]{1,0:T(2,128)(2,1)S(1)} %collective-permute-done.4), channel_id=1, source_target_pairs={{0,7},{1,0},{2,1},{3,2},{4,3},{5,4},{6,5},{7,6},{8,15},{9,8},{10,9... | collective-permute-start | bytes 99848 | tf_op jit(solution)/shard_map/ppermute | solution.py:22
  16.2 6.6 %collective-permute-start.2 = (bf16[2,8320]{1,0:T(2,128)(2,1)S(1)}, bf16[2,8320]{1,0:T(2,128)(2,1)S(1)}, u32[]{:S(2)}, u32[]{:S(2)}) collective-permute-start(bf16[2,8320]{1,0:T(2,128)(2,1)S(1)} %collective-permute-done.1), channel_id=1, source_target_pairs={{0,1},{1,2},{2,3},{3,4},{4,5},{5,6},{6,7},{7,0},{8,9},{9,10},{10,1... | collective-permute-start | bytes 99848 | tf_op jit(solution)/shard_map/ppermute | solution.py:20
  16.2 6.9 %copy-start.1 = (bf16[16,64,512]{2,1,0:T(8,128)(2,1)S(1)}, bf16[16,64,512]{2,1,0:T(8,128)(2,1)}, u32[]{:S(2)}) copy-start(bf16[16,64,512]{2,1,0:T(8,128)(2,1)} %param.17) | copy-start | bytes 3145732
  17.4 6.8 %collective-permute-start.6 = (bf16[2,8320]{1,0:T(2,128)(2,1)S(1)}, bf16[2,8320]{1,0:T(2,128)(2,1)S(1)}, u32[]{:S(2)}, u32[]{:S(2)}) collective-permute-start(bf16[2,8320]{1,0:T(2,128)(2,1)S(1)} %collective-permute-done.5), channel_id=1, source_target_pairs={{0,7},{1,0},{2,1},{3,2},{4,3},{5,4},{6,5},{7,6},{8,15},{9,8},{10,9... | collective-permute-start | bytes 99848 | tf_op jit(solution)/shard_map/ppermute | solution.py:22
  22.8 6.6 %collective-permute-start.3 = (bf16[2,8320]{1,0:T(2,128)(2,1)S(1)}, bf16[2,8320]{1,0:T(2,128)(2,1)S(1)}, u32[]{:S(2)}, u32[]{:S(2)}) collective-permute-start(bf16[2,8320]{1,0:T(2,128)(2,1)S(1)} %collective-permute-done.2), channel_id=1, source_target_pairs={{0,1},{1,2},{2,3},{3,4},{4,5},{5,6},{6,7},{7,0},{8,9},{9,10},{10,1... | collective-permute-start | bytes 99848 | tf_op jit(solution)/shard_map/ppermute | solution.py:20
  32.9 1.0 %copy-start.3 = (bf16[8,32,512]{2,1,0:T(8,128)(2,1)S(1)}, bf16[8,32,512]{2,1,0:T(8,128)(2,1)}, u32[]{:S(2)}) copy-start(bf16[8,32,512]{2,1,0:T(8,128)(2,1)} %param.14) | copy-start | bytes 786436
  36.3 1.2 %copy-start.2 = (bf16[1024,4,128]{2,1,0:T(4,128)(2,1)S(1)}, bf16[1024,4,128]{2,1,0:T(4,128)(2,1)}, u32[]{:S(2)}) copy-start(bf16[1024,4,128]{2,1,0:T(4,128)(2,1)} %reshape.132) | copy-start | bytes 3145732
  39.5 2.8 %copy-start.8 = (bf16[2,2,512]{2,1,0:T(2,128)(2,1)S(1)}, bf16[2,2,512]{2,1,0:T(2,128)(2,1)}, u32[]{:S(2)}) copy-start(bf16[2,2,512]{2,1,0:T(2,128)(2,1)} %param.20) | copy-start | bytes 12292
  39.5 3.3 %copy-start.5 = (bf16[2,2,512]{2,1,0:T(2,128)(2,1)S(1)}, bf16[2,2,512]{2,1,0:T(2,128)(2,1)}, u32[]{:S(2)}) copy-start(bf16[2,2,512]{2,1,0:T(2,128)(2,1)} %param.21) | copy-start | bytes 12292
  39.5 21.9 %all-to-all-start = ((f32[32,33,128]{2,1,0:T(8,128)}), f32[32,33,128]{2,1,0:T(8,128)S(1)}, u32[]{:S(2)}, u32[]{:S(2)}) async-start(f32[32,33,128]{2,1,0:T(8,128)} %copy.96), calls=%async_computation | async-start | bytes 1310720 | tf_op jit(solution)/shard_map/all_to_all | solution.py:134
